TPU v7x, 128 devices: a whole 4x4x4 slice. The times are simulated.
128 devices in a mesh: wide: 16 (over z, y), col: 8 (over x, core).
Axes of the slice: x: 4, y: 4, z: 4, core: 2. Of those that a mesh axis runs over, the one named last changes fastest.
Arguments:
- z_root: float32 [512, 16384], P('col', 'wide'), may hold values from -6 to 6
- z_child: float32 [512, 2, 8192], P('col', None, 'wide'), may hold values from -6 to 6
- z_grand: float32 [512, 4, 4096], P('col', None, 'wide'), may hold values from -6 to 6
- inv_root: float32 [16384, 16384], P('wide', 'col'), as said below
- inv_child: float32 [2, 8192, 8192], P(None, 'wide', 'col'), as said below
- inv_grand: float32 [4, 4096, 4096], P(None, 'wide', 'col'), as said below
- panel_child: float32 [2, 4096, 8192], P(None, 'col', 'wide'), may hold values from -0.046875 to 0.046875
- panel_grand: float32 [4, 2048, 4096], P(None, 'col', 'wide'), may hold values from -0.0625 to 0.0625
- anc_child: int32 [2, 32], P(None, 'col'), may hold values from 0 to 127, as said below
- anc_grand: int32 [4, 16], P(None, 'col'), may hold values from 0 to 255, as said below
Outputs:
- x_root: float32 [512, 16384], P('wide', 'col')
- x_child: float32 [512, 2, 8192], P('wide', None, 'col')
- x_grand: float32 [512, 4, 4096], P('wide', None, 'col')
Inputs may be any that keep to these rules, and one draw needn't show every extreme that they name: inv_root is lower triangular with a positive diagonal (entries above the diagonal are zero). Each inv_child[k] is lower triangular with a positive diagonal. Each inv_grand[g] is lower triangular with a positive diagonal. `anc_child`: each row lists distinct blocks in rising order and always names block 0 and block 127. `anc_grand`: row g lists 2048 // 256 distinct root blocks in rising order, block 0 and block 127 among them, then as many distinct blocks of child g // 2 (numbered 16384 // 128 + (g // 2) * 64 onwards) in rising order, its first and its last among them.
All inputs are finite; a program needn't handle non-finite values.
Results may differ from a plain program's by a relative error of at most 0.000096.
Values sent between devices are 32-bit elements; how exact they have to be, the bound alone decides.
No kernel may reach another device: no remote copies, remote signals or barrier semaphores. Data moves between devices by JAX's collectives and lax.ppermute only.
A program may use at most 128 MiB of HBM per device.

v0:
```python
import jax
import jax.numpy as jnp
from jax import lax
from jax.sharding import PartitionSpec as P

BLK = 128
PRECISE = lax.Precision.HIGHEST


def pick_blocks(source_rows, blocks):
    leading = source_rows.shape[0]
    tiled = source_rows.reshape(leading, source_rows.shape[1] // BLK, BLK)
    selected = jnp.take(tiled, blocks.reshape(-1), axis=1)
    return selected.reshape(leading, blocks.shape[0], blocks.shape[1] * BLK)


def spread_rhs(local_part):
    return lax.all_gather(local_part, "col", axis=0, tiled=True)


def solve_terms(right_rows, inverse):
    return lax.psum_scatter(
        jnp.einsum(
            "ski,kij->skj",
            right_rows,
            inverse,
            precision=PRECISE,
            preferred_element_type=jnp.float32,
        ),
        "wide",
        scatter_dimension=0,
        tiled=True,
    )


def spread_solved(solved_local):
    gathered = lax.all_gather(solved_local, "col", axis=2, tiled=True)
    return gathered.reshape(gathered.shape[0], -1)


def fetch_ancestors(source_rows, blocks):
    return lax.all_gather(pick_blocks(source_rows, blocks), "wide", axis=0, tiled=True)


def finish_level(z_local, inverse, partial_value):
    summed = lax.psum(partial_value, "col")
    right_side = spread_rhs(z_local) - summed
    solved = solve_terms(right_side, inverse)
    return solved


def per_device(
    z_root,
    z_child,
    z_grand,
    inv_root,
    inv_child,
    inv_grand,
    panel_child,
    panel_grand,
    anc_child,
    anc_grand,
):
    root_right = spread_rhs(z_root[:, None, :])
    root_solved = solve_terms(root_right, inv_root[None])
    x_root = root_solved[:, 0, :]
    root_rows = spread_solved(root_solved)
    near_rows = fetch_ancestors(root_rows, anc_child)
    partial_value = jnp.einsum(
        "ska,kaj->skj",
        near_rows,
        panel_child,
        precision=PRECISE,
        preferred_element_type=jnp.float32,
    )
    x_child = finish_level(z_child, inv_child, partial_value)
    child_rows = spread_solved(x_child)
    solved_all = jnp.concatenate([root_rows, child_rows], axis=1)
    far_rows = fetch_ancestors(solved_all, anc_grand)
    partial_grand = jnp.einsum(
        "sga,gaj->sgj", far_rows, panel_grand, precision=PRECISE, preferred_element_type=jnp.float32
    )
    x_grand = finish_level(z_grand, inv_grand, partial_grand)
    return (x_root, x_child, x_grand)


def solution(mesh):
    in_specs = (
        P("col", "wide"),
        P("col", None, "wide"),
        P("col", None, "wide"),
        P("wide", "col"),
        P(None, "wide", "col"),
        P(None, "wide", "col"),
        P(None, "col", "wide"),
        P(None, "col", "wide"),
        P(None, "col"),
        P(None, "col"),
    )
    out_specs = (P("wide", "col"), P("wide", None, "col"), P("wide", None, "col"))
    return jax.shard_map(
        per_device, mesh=mesh, in_specs=in_specs, out_specs=out_specs, check_vma=False
    )
```

profile of v0, /device:TPU:0, one launch (start us, length us, event | category | flops | bytes accessed | tf_op | source)
XLA Modules:
  0.0 726.2 jit_solution(2255232434404925078)
XLA Ops:
  7.2 0.0 all-gather.21.cloned.1.call-start
  7.2 0.7 all-gather.21.cloned.1.call-update
  7.9 0.0 all-reduce.9.cloned.1.call-start
  8.0 29.4 %all-gather.21.cloned.1.call-done = f32[512,1024]{1,0:T(8,128)} async-done(((f32[64,1024]{1,0:T(8,128)}), f32[512,1024]{1,0:T(8,128)}) %all-gather.21.cloned.1.call-update) | async-done | bytes 2097168 | tf_op jit(solution)/shard_map/all_gather | solution.py:18
  37.4 30.4 %convolution_bitcast_fusion = f32[512,1,2048]{0,2,1:T(8,128)} fusion(f32[1024,2048]{1,0:T(8,128)} %param.13, f32[512,1024]{1,0:T(8,128)} %all-gather.21.cloned.1.call-done), kind=kOutput, calls=%fused_computation.3 | convolution fusion | flops 12884901888 | bytes 14680064 | tf_op jit(solution)/shard_map/ski,kij->skj/dot_general | solution.py:23
  67.8 11.0 %copy.75 = f32[512,1,2048]{2,1,0:T(1,128)} copy(f32[512,1,2048]{0,2,1:T(8,128)} %convolution_bitcast_fusion) | data formatting | bytes 8388608 | tf_op jit(solution)/shard_map/ski,kij->skj/transpose | solution.py:23
  78.8 0.0 all-reduce.9.cloned.1.call-update
  78.8 0.0 all-gather.11.cloned.1.call-start
  78.9 0.6 copy-done.8
  79.5 0.6 dynamic-slice
  80.7 102.2 %all-reduce.9.cloned.1.call-done = f32[512,1,2048]{2,1,0:T(1,128)} async-done(((f32[512,1,2048]{2,1,0:T(1,128)}), f32[512,1,2048]{2,1,0:T(1,128)}) %all-reduce.9.cloned.1.call-update) | async-done | bytes 4194320
  183.0 1.7 constant_dynamic-slice_fusion
  184.6 0.0 all-gather.11.cloned.1.call-update
  184.7 0.0 all-gather.13.cloned.1.call-start
  184.7 0.1 reshape.104
  184.8 0.1 broadcast_bitcast_fusion.1
  184.9 25.1 %all-gather.11.cloned.1.call-done = f32[32,1,16384]{2,1,0:T(1,128)} async-done(((f32[32,1,2048]{2,1,0:T(1,128)}), f32[32,1,16384]{2,1,0:T(1,128)}) %all-gather.11.cloned.1.call-update) | async-done | bytes 2097168 | tf_op jit(solution)/shard_map/all_gather | solution.py:37
  210.0 4.2 copy.77
  214.3 2.1 gather_fusion
  216.4 0.1 copy.78
  216.5 0.1 gather.13
  216.6 0.7 copy_select_fusion.1
  217.3 0.0 all-gather.13.cloned.1.call-update
  217.3 0.0 all-gather.9.cloned.1.call-start
  217.3 0.8 copy.76
  218.1 0.0 all-gather.9.cloned.1.call-update
  218.1 0.0 all-reduce.5.cloned.1.call-start
  218.2 44.9 %all-gather.13.cloned.1.call-done = f32[512,2,512]{2,0,1:T(8,128)} async-done(((f32[32,2,512]{2,0,1:T(8,128)}), f32[512,2,512]{2,0,1:T(8,128)}) %all-gather.13.cloned.1.call-update) | async-done | bytes 2097168 | tf_op jit(solution)/shard_map/all_gather | solution.py:42
  263.0 7.0 convolution_bitcast_fusion.4
  270.1 0.0 all-reduce.5.cloned.1.call-update
  270.1 0.0 reduce-scatter.3.cloned.1.call-start
  270.1 19.4 %all-gather.9.cloned.1.call-done = f32[512,2,512]{2,0,1:T(8,128)} async-done(((f32[64,2,512]{2,0,1:T(8,128)}), f32[512,2,512]{2,0,1:T(8,128)}) %all-gather.9.cloned.1.call-update) | async-done | bytes 2097168 | tf_op jit(solution)/shard_map/all_gather | solution.py:18
  289.6 68.2 %all-reduce.5.cloned.1.call-done = f32[512,2,512]{2,0,1:T(8,128)} async-done(((f32[512,2,512]{2,0,1:T(8,128)}), f32[512,2,512]{2,0,1:T(8,128)}) %all-reduce.5.cloned.1.call-update) | async-done | bytes 2097168 | tf_op jit(solution)/shard_map/psum | solution.py:46
  357.8 12.2 %convolution_bitcast_fusion.2 = f32[512,2,1024]{2,0,1:T(8,128)} fusion(f32[2,512,1024]{2,1,0:T(8,128)} %param.14, f32[512,2,512]{2,0,1:T(8,128)} %all-gather.9.cloned.1.call-done, f32[512,2,512]{2,0,1:T(8,128)} %all-reduce.5.cloned.1.call-done), kind=kOutput, calls=%fused_computation.5 | convolution fusion | flops 6442975232 | bytes 12582912 | tf_op jit(solution)/shard_map/ski,kij->skj/dot_general | solution.py:23
  370.0 0.0 reduce-scatter.3.cloned.1.call-update
  370.0 0.0 all-gather.17.cloned.1.call-start
  370.1 77.5 %reduce-scatter.3.cloned.1.call-done = f32[32,2,1024]{2,0,1:T(8,128)} async-done(((f32[512,2,1024]{2,0,1:T(8,128)}), f32[32,2,1024]{2,0,1:T(8,128)}) %reduce-scatter.3.cloned.1.call-update) | async-done | bytes 262160 | tf_op jit(solution)/shard_map/reduce_scatter | solution.py:22
  447.6 0.0 all-gather.19.cloned.1.call-start
  447.6 0.1 copy.84
  447.7 0.1 reshape.105
  447.9 0.1 broadcast_bitcast_fusion
  447.9 25.8 %all-gather.17.cloned.1.call-done = f32[32,2,8192]{2,0,1:T(8,128)} async-done(((f32[32,2,1024]{2,0,1:T(8,128)}), f32[32,2,8192]{2,0,1:T(8,128)}) %all-gather.17.cloned.1.call-update) | async-done | bytes 2097168 | tf_op jit(solution)/shard_map/all_gather | solution.py:37
  473.7 4.6 copy.81
  478.3 4.0 concatenate.6
  482.3 3.0 copy.83
  485.3 2.4 pad_maximum_fusion
  487.7 2.8 gather_fusion.1
  490.5 0.1 copy.85
  490.6 0.1 gather.15
  490.7 0.7 copy_select_fusion
  491.4 0.0 all-gather.15.cloned.1.call-start
  491.4 1.7 copy.80
  493.2 0.0 all-reduce.7.cloned.1.call-start
  493.2 43.9 %all-gather.19.cloned.1.call-done = f32[512,4,256]{2,0,1:T(8,128)} async-done(((f32[32,4,256]{2,0,1:T(8,128)}), f32[512,4,256]{2,0,1:T(8,128)}) %all-gather.19.cloned.1.call-update) | async-done | bytes 2097168 | tf_op jit(solution)/shard_map/all_gather | solution.py:42
  537.1 4.9 convolution_bitcast_fusion.3
  542.0 0.0 reduce-scatter.5.cloned.1.call-start
  542.1 21.7 %all-gather.15.cloned.1.call-done = f32[512,4,256]{2,0,1:T(8,128)} async-done(((f32[64,4,256]{2,0,1:T(8,128)}), f32[512,4,256]{2,0,1:T(8,128)}) %all-gather.15.cloned.1.call-update) | async-done | bytes 2097168 | tf_op jit(solution)/shard_map/all_gather | solution.py:18
  563.8 68.5 %all-reduce.7.cloned.1.call-done = f32[512,4,256]{2,0,1:T(8,128)} async-done(((f32[512,4,256]{2,0,1:T(8,128)}), f32[512,4,256]{2,0,1:T(8,128)}) %all-reduce.7.cloned.1.call-update) | async-done | bytes 2097168 | tf_op jit(solution)/shard_map/psum | solution.py:46
  632.3 7.8 %convolution_bitcast_fusion.1 = f32[512,4,512]{2,0,1:T(8,128)} fusion(f32[4,256,512]{2,1,0:T(8,128)S(1)} %copy-done, f32[512,4,256]{2,0,1:T(8,128)} %all-gather.15.cloned.1.call-done, f32[512,4,256]{2,0,1:T(8,128)} %all-reduce.7.cloned.1.call-done), kind=kOutput, calls=%fused_computation.4 | convolution fusion | flops 3221749760 | bytes 10485760 | tf_op jit(solution)/shard_map/ski,kij->skj/dot_general | solution.py:23
  640.0 0.9 copy-done.2
  641.0 0.8 copy.95
  641.8 0.9 copy.87
  642.7 74.9 %reduce-scatter.5.cloned.1.call-done = f32[32,4,512]{2,0,1:T(8,128)} async-done(((f32[512,4,512]{2,0,1:T(8,128)}), f32[32,4,512]{2,0,1:T(8,128)}) %reduce-scatter.5.cloned.1.call-update) | async-done | bytes 262160 | tf_op jit(solution)/shard_map/reduce_scatter | solution.py:22
  717.6 1.8 copy.88
  (28 shorter events, 0.2 us)
Async XLA Ops:
  7.2 625.1 %copy-start = (f32[4,256,512]{2,1,0:T(8,128)S(1)}, f32[4,256,512]{2,1,0:T(8,128)}, u32[]{:S(2)}) copy-start(f32[4,256,512]{2,1,0:T(8,128)} %param.15) | copy-start | bytes 6291460
  7.2 30.2 %all-gather.21.cloned.1.call-start = ((), (), s32[]{:S(2)}) async-start(), calls=%async_computation.12 | async-start | bytes 2359296 | tf_op jit(solution)/shard_map/all_gather | solution.py:18
  7.9 175.0 %all-reduce.9.cloned.1.call-start = ((), (), s32[]{:S(2)}) async-start(), calls=%async_computation.13 | async-start | bytes 8388608
  78.8 0.7 copy-start.8
  78.8 105.9 %copy-start.7 = (s32[2,4]{1,0:T(2,128)S(1)}, s32[2,4]{1,0:T(2,128)}, u32[]{:S(2)}) copy-start(s32[2,4]{1,0:T(2,128)} %param.18) | copy-start | bytes 100
  78.8 131.2 %all-gather.11.cloned.1.call-start = ((), (), s32[]{:S(2)}) async-start(), calls=%async_computation.3 | async-start | bytes 2359296 | tf_op jit(solution)/shard_map/all_gather | solution.py:37
  184.7 78.4 %all-gather.13.cloned.1.call-start = ((), (), s32[]{:S(2)}) async-start(), calls=%async_computation.4 | async-start | bytes 2228224 | tf_op jit(solution)/shard_map/all_gather | solution.py:42
  210.0 7.3 %copy-start.5 = (f32[64,2,512]{2,1,0:T(2,128)S(1)}, f32[64,2,512]{2,1,0:T(2,128)}, u32[]{:S(2)}) copy-start(f32[64,2,512]{2,1,0:T(2,128)} %param.11) | copy-start | bytes 786436
  217.3 72.3 %all-gather.9.cloned.1.call-start = ((), (), s32[]{:S(2)}) async-start(), calls=%async_computation.2 | async-start | bytes 2359296 | tf_op jit(solution)/shard_map/all_gather | solution.py:18
  218.1 139.7 %all-reduce.5.cloned.1.call-start = ((), (), s32[]{:S(2)}) async-start(), calls=%async_computation.5 | async-start | bytes 4194304 | tf_op jit(solution)/shard_map/psum | solution.py:46
  270.1 177.5 %reduce-scatter.3.cloned.1.call-start = ((), (), s32[]{:S(2)}) async-start(), calls=%async_computation.6 | async-start | bytes 4456448 | tf_op jit(solution)/shard_map/reduce_scatter | solution.py:22
  370.0 77.7 %copy-start.6 = (s32[4,2]{0,1:T(2,128)S(1)}, s32[4,2]{0,1:T(2,128)}, u32[]{:S(2)}) copy-start(s32[4,2]{0,1:T(2,128)} %param.19) | copy-start | bytes 100
  370.0 103.7 %all-gather.17.cloned.1.call-start = ((), (), s32[]{:S(2)}) async-start(), calls=%async_computation.8 | async-start | bytes 2359296 | tf_op jit(solution)/shard_map/all_gather | solution.py:37
  447.6 89.6 %all-gather.19.cloned.1.call-start = ((), (), s32[]{:S(2)}) async-start(), calls=%async_computation.9 | async-start | bytes 2228224 | tf_op jit(solution)/shard_map/all_gather | solution.py:42
  482.3 3.0 copy-start.1
  487.7 49.5 %copy-start.3 = (f32[4,256,256]{2,1,0:T(8,128)S(1)}, f32[4,256,256]{2,1,0:T(8,128)}, u32[]{:S(2)}) copy-start(f32[4,256,256]{2,1,0:T(8,128)} %param.17) | copy-start | bytes 3145732
  491.4 72.4 %all-gather.15.cloned.1.call-start = ((), (), s32[]{:S(2)}) async-start(), calls=%async_computation.7 | async-start | bytes 2359296 | tf_op jit(solution)/shard_map/all_gather | solution.py:18
  493.2 139.1 %all-reduce.7.cloned.1.call-start = ((), (), s32[]{:S(2)}) async-start(), calls=%async_computation.10 | async-start | bytes 4194304 | tf_op jit(solution)/shard_map/psum | solution.py:46
  542.0 175.5 %reduce-scatter.5.cloned.1.call-start = ((), (), s32[]{:S(2)}) async-start(), calls=%async_computation.11 | async-start | bytes 4456448 | tf_op jit(solution)/shard_map/reduce_scatter | solution.py:22
  640.0 0.9 copy-start.2
  640.0 1.7 copy-start.4
Sparse Core Ops, SparseCore 0:
  9.7 27.5 all-gather.20
  79.0 103.9 all-reduce.8
  185.2 24.7 all-gather.10
  217.4 45.5 all-gather.12
  265.2 24.3 all-gather.8
  291.8 65.9 all-reduce.4
  370.1 77.3 reduce-scatter.2
  449.4 24.3 all-gather.16
  491.5 45.5 all-gather.18
  539.4 24.3 all-gather.14
  566.3 65.9 all-reduce.6
  640.2 77.3 reduce-scatter.4
where the time goes:
time: 727 us; the launch traced here: 726 us
  waiting for transfers between devices  602 us (83%)
  matrix products  62.3 us (9%)
  local copies, waits for them, and re-layouts  42.2 us (6%)
  between operations  15 us (2%)
    reduce_scatter x2, waiting for transfers between devices, solve_terms(): lax.psum_scatter(jnp.einsum('ski,kij->skj', right_rows, inverse, precisio...  152 us
    psum x2, waiting for transfers between devices, finish_level(): summed = lax.psum(partial_value, 'col')  137 us
    unnamed x13, waiting for transfers between devices  103 us
    all_gather x2, waiting for transfers between devices, fetch_ancestors(): lax.all_gather(pick_blocks(source_rows, blocks), 'wide', axis=0, tiled=True)  88.8 us
    all_gather x3, waiting for transfers between devices, spread_rhs(): return lax.all_gather(local_part, 'col', axis=0, tiled=True)  70.5 us
    all_gather x2, waiting for transfers between devices, spread_solved(): gathered = lax.all_gather(solved_local, 'col', axis=2, tiled=True)  50.9 us
    dot_general x3, matrix products, solve_terms(): jnp.einsum('ski,kij->skj', right_rows, inverse, precision=PRECISE, prefer...  50.4 us
  transfers between devices with their start and end apart: 12, of which 12 were waited for; matrix products, arithmetic and copies ran while one was open for 2% of the time, Pallas kernels for 0%

commit v1 on v0

--- a/solution.py
+++ b/solution.py
@@ -43,7 +43,7 @@
 
 
 def finish_level(z_local, inverse, partial_value):
-    summed = lax.psum(partial_value, "col")
+    summed = jnp.sum(lax.all_gather(partial_value, "col"), axis=0)
     right_side = spread_rhs(z_local) - summed
     solved = solve_terms(right_side, inverse)
     return solved

time: 727 us -> 775 us (1.066)
  waiting for transfers between devices: 602 us -> 634 us
  other arithmetic: 3.81 us -> 21.7 us
    all_gather x0 -> x2, waiting for transfers between devices: none -> 167 us  [finish_level(): summed = jnp.sum(lax.all_gather(partial_value, 'col'), axis=0)]
    psum x2 -> x0, waiting for transfers between devices: 137 us -> none  [finish_level(): summed = lax.psum(partial_value, 'col')]
    reduce_sum x0 -> x2, other arithmetic: none -> 17.9 us  [finish_level(): summed = jnp.sum(lax.all_gather(partial_value, 'col'), axis=0)]
  transfers between devices with their start and end apart: 12 -> 12, of which waited for: 12 -> 12; matrix products, arithmetic and copies ran while one was open for 2% -> 3% of each run, Pallas kernels for 0% -> 0%
where the time goes in v1:
time: 775 us; the launch traced here: 774 us
  waiting for transfers between devices  634 us (82%)
  matrix products  63.3 us (8%)
  local copies, waits for them, and re-layouts  39.6 us (5%)
  other arithmetic  21.7 us (3%)
  between operations  15 us (2%)
    all_gather x2, waiting for transfers between devices, finish_level(): summed = jnp.sum(lax.all_gather(partial_value, 'col'), axis=0)  167 us
    reduce_scatter x2, waiting for transfers between devices, solve_terms(): lax.psum_scatter(jnp.einsum('ski,kij->skj', right_rows, inverse, precisio...  154 us
    unnamed x13, waiting for transfers between devices  104 us
    all_gather x2, waiting for transfers between devices, fetch_ancestors(): lax.all_gather(pick_blocks(source_rows, blocks), 'wide', axis=0, tiled=True)  91.4 us
    all_gather x3, waiting for transfers between devices, spread_rhs(): return lax.all_gather(local_part, 'col', axis=0, tiled=True)  66.5 us
    dot_general x3, matrix products, solve_terms(): jnp.einsum('ski,kij->skj', right_rows, inverse, precision=PRECISE, prefer...  51.3 us
    all_gather x2, waiting for transfers between devices, spread_solved(): gathered = lax.all_gather(solved_local, 'col', axis=2, tiled=True)  50.7 us
    reduce_sum x2, other arithmetic, finish_level(): summed = jnp.sum(lax.all_gather(partial_value, 'col'), axis=0)  17.9 us
  transfers between devices with their start and end apart: 12, of which 12 were waited for; matrix products, arithmetic and copies ran while one was open for 3% of the time, Pallas kernels for 0%

profile of v1, /device:TPU:0, one launch (start us, length us, event | category | flops | bytes accessed | tf_op | source)
XLA Modules:
  0.0 774.3 jit_solution(989977373798437823)
XLA Ops:
  7.2 0.0 all-gather.25.cloned.1.call-start
  7.2 0.7 all-gather.25.cloned.1.call-update
  7.9 0.0 all-reduce.3.cloned.1.call-start
  8.0 29.4 %all-gather.25.cloned.1.call-done = f32[512,1024]{1,0:T(8,128)} async-done(((f32[64,1024]{1,0:T(8,128)}), f32[512,1024]{1,0:T(8,128)}) %all-gather.25.cloned.1.call-update) | async-done | bytes 2097168 | tf_op jit(solution)/shard_map/all_gather | solution.py:18
  37.4 30.4 %convolution_bitcast_fusion = f32[512,1,2048]{0,2,1:T(8,128)} fusion(f32[1024,2048]{1,0:T(8,128)} %param.13, f32[512,1024]{1,0:T(8,128)} %all-gather.25.cloned.1.call-done), kind=kOutput, calls=%fused_computation.3 | convolution fusion | flops 12884901888 | bytes 14680064 | tf_op jit(solution)/shard_map/ski,kij->skj/dot_general | solution.py:23
  67.8 11.0 %copy.56 = f32[512,1,2048]{2,1,0:T(1,128)} copy(f32[512,1,2048]{0,2,1:T(8,128)} %convolution_bitcast_fusion) | data formatting | bytes 8388608 | tf_op jit(solution)/shard_map/ski,kij->skj/transpose | solution.py:23
  78.8 0.0 all-reduce.3.cloned.1.call-update
  78.9 0.0 all-gather.15.cloned.1.call-start
  78.9 0.6 copy-done.7
  79.5 0.6 dynamic-slice
  80.7 102.2 %all-reduce.3.cloned.1.call-done = f32[512,1,2048]{2,1,0:T(1,128)} async-done(((f32[512,1,2048]{2,1,0:T(1,128)}), f32[512,1,2048]{2,1,0:T(1,128)}) %all-reduce.3.cloned.1.call-update) | async-done | bytes 4194320
  183.0 1.7 constant_dynamic-slice_fusion
  184.7 0.0 all-gather.17.cloned.1.call-start
  184.7 0.1 reshape.104
  184.8 0.1 broadcast_bitcast_fusion.1
  184.9 25.1 %all-gather.15.cloned.1.call-done = f32[32,1,16384]{2,1,0:T(1,128)} async-done(((f32[32,1,2048]{2,1,0:T(1,128)}), f32[32,1,16384]{2,1,0:T(1,128)}) %all-gather.15.cloned.1.call-update) | async-done | bytes 2097168 | tf_op jit(solution)/shard_map/all_gather | solution.py:37
  210.1 4.1 copy.57
  214.2 2.1 gather_fusion
  216.4 0.1 copy.58
  216.4 0.1 gather.13
  216.5 0.7 copy_select_fusion.1
  217.2 0.0 all-gather.27.cloned.1.call-start
  217.3 45.7 %all-gather.17.cloned.1.call-done = f32[512,2,512]{2,0,1:T(8,128)} async-done(((f32[32,2,512]{2,0,1:T(8,128)}), f32[512,2,512]{2,0,1:T(8,128)}) %all-gather.17.cloned.1.call-update) | async-done | bytes 2097168 | tf_op jit(solution)/shard_map/all_gather | solution.py:42
  263.0 7.1 convolution_bitcast_fusion.4
  270.1 0.0 all-gather.27.cloned.1.call-update
  270.1 0.0 all-gather.13.cloned.1.call-start
  270.2 0.5 all-gather.13.cloned.1.call-update
  270.7 0.0 reduce-scatter.3.cloned.1.call-start
  270.7 83.6 %all-gather.27.cloned.1.call-done = f32[4096,2,512]{2,0,1:T(8,128)} async-done(((f32[512,2,512]{2,0,1:T(8,128)}), f32[4096,2,512]{2,0,1:T(8,128)}) %all-gather.27.cloned.1.call-update) | async-done | bytes 16777232 | tf_op jit(solution)/shard_map/all_gather | solution.py:46
  354.4 9.4 %reduce_sum.18 = f32[512,2,512]{2,0,1:T(8,128)} reduce(f32[8,512,2,512]{3,1,0,2:T(8,128)} %bitcast.41, f32[]{:T(128)} %constant.29.clone.1), dimensions={0}, to_apply=%region_1.2 | reduce | flops 3670016 | bytes 18874372 | tf_op jit(solution)/shard_map/reduce_sum | solution.py:46
  363.8 17.9 %all-gather.13.cloned.1.call-done = f32[512,2,512]{2,1,0:T(2,128)} async-done(((f32[64,2,512]{2,1,0:T(2,128)}), f32[512,2,512]{2,1,0:T(2,128)}) %all-gather.13.cloned.1.call-update) | async-done | bytes 2097168 | tf_op jit(solution)/shard_map/all_gather | solution.py:18
  381.8 12.4 %convolution_bitcast_fusion.2 = f32[512,2,1024]{2,0,1:T(8,128)} fusion(f32[2,512,1024]{2,1,0:T(8,128)} %param.14, f32[512,2,512]{2,0,1:T(8,128)} %reduce_sum.18, f32[512,2,512]{2,1,0:T(2,128)} %all-gather.13.cloned.1.call-done), kind=kOutput, calls=%fused_computation.5 | convolution fusion | flops 6442975232 | bytes 12582912 | tf_op jit(solution)/shard_map/ski,kij->skj/dot_general | solution.py:23
  394.2 0.0 reduce-scatter.3.cloned.1.call-update
  394.2 0.0 all-gather.21.cloned.1.call-start
  394.3 78.2 %reduce-scatter.3.cloned.1.call-done = f32[32,2,1024]{2,0,1:T(8,128)} async-done(((f32[512,2,1024]{2,0,1:T(8,128)}), f32[32,2,1024]{2,0,1:T(8,128)}) %reduce-scatter.3.cloned.1.call-update) | async-done | bytes 262160 | tf_op jit(solution)/shard_map/reduce_scatter | solution.py:22
  472.5 0.3 all-gather.23.cloned.1.call-start
  472.8 0.1 copy.64
  472.9 0.1 reshape.105
  473.0 0.1 broadcast_bitcast_fusion
  473.0 25.6 %all-gather.21.cloned.1.call-done = f32[32,2,8192]{2,0,1:T(8,128)} async-done(((f32[32,2,1024]{2,0,1:T(8,128)}), f32[32,2,8192]{2,0,1:T(8,128)}) %all-gather.21.cloned.1.call-update) | async-done | bytes 2097168 | tf_op jit(solution)/shard_map/all_gather | solution.py:37
  498.6 4.5 copy.61
  503.2 4.0 concatenate.6
  507.2 3.0 copy.63
  510.2 2.4 pad_maximum_fusion
  512.6 2.7 gather_fusion.1
  515.3 0.1 copy.65
  515.4 0.1 gather.15
  515.5 0.7 copy_select_fusion
  516.2 0.0 all-gather.23.cloned.1.call-update
  516.2 0.0 all-gather.29.cloned.1.call-start
  516.2 45.7 %all-gather.23.cloned.1.call-done = f32[512,4,256]{2,0,1:T(8,128)} async-done(((f32[32,4,256]{2,0,1:T(8,128)}), f32[512,4,256]{2,0,1:T(8,128)}) %all-gather.23.cloned.1.call-update) | async-done | bytes 2097168 | tf_op jit(solution)/shard_map/all_gather | solution.py:42
  562.0 4.9 convolution_bitcast_fusion.3
  566.9 0.0 all-gather.19.cloned.1.call-start
  566.9 0.7 all-gather.19.cloned.1.call-update
  567.6 0.0 reduce-scatter.5.cloned.1.call-start
  567.6 83.5 %all-gather.29.cloned.1.call-done = f32[4096,4,256]{2,0,1:T(8,128)} async-done(((f32[512,4,256]{2,0,1:T(8,128)}), f32[4096,4,256]{2,0,1:T(8,128)}) %all-gather.29.cloned.1.call-update) | async-done | bytes 16777232 | tf_op jit(solution)/shard_map/all_gather | solution.py:46
  651.1 8.4 %reduce_sum.19 = f32[512,4,256]{2,0,1:T(8,128)} reduce(f32[8,512,4,256]{3,1,0,2:T(8,128)} %bitcast.40, f32[]{:T(128)} %constant.29.clone.1), dimensions={0}, to_apply=%region_3.4 | reduce | flops 3670016 | bytes 18874372 | tf_op jit(solution)/shard_map/reduce_sum | solution.py:46
  659.6 19.2 %all-gather.19.cloned.1.call-done = f32[512,4,256]{2,1,0:T(4,128)} async-done(((f32[64,4,256]{2,1,0:T(4,128)}), f32[512,4,256]{2,1,0:T(4,128)}) %all-gather.19.cloned.1.call-update) | async-done | bytes 2097168 | tf_op jit(solution)/shard_map/all_gather | solution.py:18
  678.8 8.5 %convolution_bitcast_fusion.1 = f32[512,4,512]{2,0,1:T(8,128)} fusion(f32[4,256,512]{2,1,0:T(8,128)S(1)} %copy-done, f32[512,4,256]{2,0,1:T(8,128)} %reduce_sum.19, f32[512,4,256]{2,1,0:T(4,128)} %all-gather.19.cloned.1.call-done), kind=kOutput, calls=%fused_computation.4 | convolution fusion | flops 3221749760 | bytes 10485760 | tf_op jit(solution)/shard_map/ski,kij->skj/dot_general | solution.py:23
  687.3 0.9 copy-done.2
  688.2 0.8 copy.80
  689.0 0.9 copy.68
  689.9 75.7 %reduce-scatter.5.cloned.1.call-done = f32[32,4,512]{2,0,1:T(8,128)} async-done(((f32[512,4,512]{2,0,1:T(8,128)}), f32[32,4,512]{2,0,1:T(8,128)}) %reduce-scatter.5.cloned.1.call-update) | async-done | bytes 262160 | tf_op jit(solution)/shard_map/reduce_scatter | solution.py:22
  765.6 1.8 copy.69
  (26 shorter events, 0.2 us)
Async XLA Ops:
  7.2 671.6 %copy-start = (f32[4,256,512]{2,1,0:T(8,128)S(1)}, f32[4,256,512]{2,1,0:T(8,128)}, u32[]{:S(2)}) copy-start(f32[4,256,512]{2,1,0:T(8,128)} %param.15) | copy-start | bytes 6291460
  7.2 30.2 %all-gather.25.cloned.1.call-start = ((), (), s32[]{:S(2)}) async-start(), calls=%async_computation.10 | async-start | bytes 2359296 | tf_op jit(solution)/shard_map/all_gather | solution.py:18
  7.9 175.1 %all-reduce.3.cloned.1.call-start = ((), (), s32[]{:S(2)}) async-start(), calls=%async_computation.13 | async-start | bytes 8388608
  78.8 0.7 copy-start.7
  78.8 105.9 %copy-start.6 = (s32[2,4]{1,0:T(2,128)S(1)}, s32[2,4]{1,0:T(2,128)}, u32[]{:S(2)}) copy-start(s32[2,4]{1,0:T(2,128)} %param.18) | copy-start | bytes 100
  78.9 131.2 %all-gather.15.cloned.1.call-start = ((), (), s32[]{:S(2)}) async-start(), calls=%async_computation.3 | async-start | bytes 2359296 | tf_op jit(solution)/shard_map/all_gather | solution.py:37
  184.7 78.3 %all-gather.17.cloned.1.call-start = ((), (), s32[]{:S(2)}) async-start(), calls=%async_computation.4 | async-start | bytes 2228224 | tf_op jit(solution)/shard_map/all_gather | solution.py:42
  217.2 137.2 %all-gather.27.cloned.1.call-start = ((), (), s32[]{:S(2)}) async-start(), calls=%async_computation.11 | async-start | bytes 18874368 | tf_op jit(solution)/shard_map/all_gather | solution.py:46
  270.1 111.7 %all-gather.13.cloned.1.call-start = ((), (), s32[]{:S(2)}) async-start(), calls=%async_computation.2 | async-start | bytes 2359296 | tf_op jit(solution)/shard_map/all_gather | solution.py:18
  270.7 201.8 %reduce-scatter.3.cloned.1.call-start = ((), (), s32[]{:S(2)}) async-start(), calls=%async_computation.5 | async-start | bytes 4456448 | tf_op jit(solution)/shard_map/reduce_scatter | solution.py:22
  394.2 78.6 %copy-start.5 = (s32[4,2]{0,1:T(2,128)S(1)}, s32[4,2]{0,1:T(2,128)}, u32[]{:S(2)}) copy-start(s32[4,2]{0,1:T(2,128)} %param.19) | copy-start | bytes 100
  394.2 104.4 %all-gather.21.cloned.1.call-start = ((), (), s32[]{:S(2)}) async-start(), calls=%async_computation.7 | async-start | bytes 2359296 | tf_op jit(solution)/shard_map/all_gather | solution.py:37
  472.5 89.5 %all-gather.23.cloned.1.call-start = ((), (), s32[]{:S(2)}) async-start(), calls=%async_computation.8 | async-start | bytes 2228224 | tf_op jit(solution)/shard_map/all_gather | solution.py:42
  507.2 3.0 copy-start.1
  510.2 51.8 %copy-start.3 = (f32[4,256,256]{2,1,0:T(8,128)S(1)}, f32[4,256,256]{2,1,0:T(8,128)}, u32[]{:S(2)}) copy-start(f32[4,256,256]{2,1,0:T(8,128)} %param.17) | copy-start | bytes 3145732
  516.2 134.9 %all-gather.29.cloned.1.call-start = ((), (), s32[]{:S(2)}) async-start(), calls=%async_computation.12 | async-start | bytes 18874368 | tf_op jit(solution)/shard_map/all_gather | solution.py:46
  566.9 111.9 %all-gather.19.cloned.1.call-start = ((), (), s32[]{:S(2)}) async-start(), calls=%async_computation.6 | async-start | bytes 2359296 | tf_op jit(solution)/shard_map/all_gather | solution.py:18
  567.6 198.0 %reduce-scatter.5.cloned.1.call-start = ((), (), s32[]{:S(2)}) async-start(), calls=%async_computation.9 | async-start | bytes 4456448 | tf_op jit(solution)/shard_map/reduce_scatter | solution.py:22
  687.3 0.9 copy-start.2
  687.3 1.7 copy-start.4
Sparse Core Ops, SparseCore 0:
  9.7 27.5 all-gather.24
  79.0 103.9 all-reduce.2
  185.3 24.7 all-gather.14
  217.4 45.5 all-gather.16
  270.2 84.0 all-gather.26
  356.0 25.7 all-gather.12
  394.3 78.0 reduce-scatter.2
  474.3 24.3 all-gather.20
  516.3 45.5 all-gather.22
  567.0 84.0 all-gather.28
  653.0 25.7 all-gather.18
  687.4 78.1 reduce-scatter.4
